TPU v7x, 32 devices: a whole 2x2x4 slice. The times are simulated.
32 devices in a mesh: grid: 8 (over z, x), mem: 4 (over y, core).
Axes of the slice: x: 2, y: 2, z: 4, core: 2. Of those that a mesh axis runs over, the one named last changes fastest.
Arguments:
- members: bfloat16 [80, 4, 16, 512], P('mem', None, 'grid'), may hold values from -0.8984375 to 0.8984375
- innovation: float32 [4, 16, 512], P(None, 'grid'), may hold values from -6 to 6
- observed_count: int32 [16, 512], P('grid'), may hold values from 0 to 3
- obs_precision: float32 [4], replicated, may hold values from 0.5 to 4
Outputs:
- recentred: bfloat16 [80, 4, 16, 512], P('mem', None, 'grid')
- increment: float32 [4, 16, 512], P('mem', 'grid')
All inputs are finite; a program needn't handle non-finite values.
Results may differ from a plain program's by a relative error of at most 0.0004.
Values may be sent and summed in bfloat16 or wider, within the bound.
No kernel may reach another device: no remote copies, remote signals or barrier semaphores. Data moves between devices by JAX's collectives and lax.ppermute only.
A program may use at most 64 MiB of HBM per device.

v0:
```python
import jax
import jax.numpy as jnp
from jax import lax
from jax.sharding import PartitionSpec as P

PASSES = 2
ITERS = 2
diffusion = 0.25


def padded(value, sides, width):
    for axis, dim in sides:
        devices, length = (lax.axis_size(axis), value.shape[dim])
        up = [(i, (i + 1) % devices) for i in range(devices - 1)]
        down = [(j, i) for i, j in up]
        last = lax.slice_in_dim(value, length - width, length, axis=dim)
        leading = lax.slice_in_dim(value, 0, width, axis=dim)
        before = lax.ppermute(last, axis, up)
        after = lax.ppermute(leading, axis, down)
        value = jnp.concatenate([before, value, after], axis=dim)
    return value


def smooth(field):
    for sweep_index in range(PASSES):
        extended = padded(field, (("grid", 2),), 1)
        centre = extended[:, :, 1:-1]
        field = centre + diffusion * (extended[:, :, :-2] + extended[:, :, 2:] - 2.0 * centre)
    for sweep_index in range(PASSES):
        field = field + diffusion * (jnp.roll(field, 1, 3) + jnp.roll(field, -1, 3) - 2.0 * field)
    return field


def member_total(product):
    summed = jnp.sum(product, axis=0)
    return summed


def norm_of(residual):
    return lax.psum(jnp.sum(residual * residual), ("grid", "mem"))


def local(members, innovation, observed_count, obs_precision):
    mem_index = lax.axis_index("mem")
    level_share = members.shape[1] // lax.axis_size("mem")
    perturbed = lax.all_to_all(members, "mem", split_axis=1, concat_axis=0, tiled=True)
    precision = lax.dynamic_slice_in_dim(obs_precision, mem_index * level_share, level_share, 0)
    local_innovation = lax.dynamic_slice_in_dim(innovation, mem_index * level_share, level_share, 0)
    weight = observed_count.astype(jnp.float32)[None] * precision[:, None, None]
    gradient = smooth(perturbed * (weight * local_innovation)[None])
    carried = jnp.zeros_like(gradient)
    residual = gradient
    direction = residual
    norm_now = norm_of(residual)
    for iteration in range(ITERS):
        smoothed = smooth(direction)
        total = member_total(perturbed * smoothed)
        back = smooth(perturbed * (weight * total)[None])
        image, smoothed = (direction + back, smoothed)
        step_size = norm_now / lax.psum(jnp.sum(direction * image), ("grid", "mem"))
        carried = carried + step_size * smoothed
        residual = residual - step_size * image
        if iteration + 1 < ITERS:
            norm_next = norm_of(residual)
            direction = residual + norm_next / norm_now * direction
            norm_now = norm_next
    increment = member_total(perturbed * carried)
    whole = lax.all_gather(increment, "mem", axis=0, tiled=True)
    recentred = (members.astype(jnp.float32) + whole[None]).astype(jnp.bfloat16)
    return (recentred, increment)


def smooth_rows(field):
    nlat = field.shape[-2]
    row = lax.broadcasted_iota(jnp.int32, (nlat, 1), 0)
    centre = jnp.where((row == 0) | (row == nlat - 1), 0.3125, 0.375)
    wide = jnp.pad(field, [(0, 0)] * (field.ndim - 2) + [(2, 2), (0, 0)])
    near = lax.slice_in_dim(wide, 1, nlat + 1, axis=-2) + lax.slice_in_dim(
        wide, 3, nlat + 3, axis=-2
    )
    far = lax.slice_in_dim(wide, 0, nlat, axis=-2) + lax.slice_in_dim(wide, 4, nlat + 4, axis=-2)
    field = centre * field + 0.25 * near + 0.0625 * far
    nlon = field.shape[-1]
    wide = jnp.concatenate([field[..., nlon - 2 :], field, field[..., :2]], axis=-1)
    near = wide[..., 1 : nlon + 1] + wide[..., 3 : nlon + 3]
    far = wide[..., :nlon] + wide[..., 4 : nlon + 4]
    return 0.375 * field + 0.25 * near + 0.0625 * far


def exchange(values, rows_for, width=128):
    devices = lax.axis_size("grid") * lax.axis_size("mem")
    nlon = rows_for.shape[-1]
    rows = rows_for.shape[1]
    lanes = [jnp.sum(v.reshape(-1, width), axis=0) for v in values]
    head = jnp.broadcast_to(jnp.concatenate(lanes), (devices, width * len(values)))
    parcel = jnp.concatenate([head, rows_for.reshape(devices, rows * nlon)], axis=1)
    got = lax.all_to_all(parcel, ("grid", "mem"), 0, 0, tiled=True)
    parts = jnp.sum(got[:, : width * len(values)].reshape(devices, len(values), width), axis=0)
    sums = jnp.dot(parts, jnp.ones((width, 128), jnp.float32), precision=lax.Precision.HIGHEST)
    received = got[:, width * len(values) :].reshape(devices, rows, nlon)
    return ([jnp.tile(sums[i : i + 1], (1, nlon // 128)) for i in range(len(values))], received)


def mem_total(part):
    mem_size = lax.axis_size("mem")
    got = lax.all_to_all(jnp.broadcast_to(part, (mem_size,) + part.shape), "mem", 0, 0, tiled=True)
    return jnp.sum(got, axis=0)


def local_by_level(members, innovation, observed_count, obs_precision):
    grid_size = lax.axis_size("grid")
    mem_size = lax.axis_size("mem")
    count, levels, rows, nlon = members.shape
    copies = grid_size // levels
    nlat = rows * grid_size
    grid_index = lax.axis_index("grid")
    mem_index = lax.axis_index("mem")
    level = grid_index // copies
    counts = jnp.broadcast_to(observed_count.astype(jnp.bfloat16), (1, levels, rows, nlon))
    high = lax.reduce_precision(innovation, exponent_bits=8, mantissa_bits=7)
    rest = innovation - high
    middle = lax.reduce_precision(rest, exponent_bits=8, mantissa_bits=7)
    low = rest - middle
    parts = jnp.stack([high, middle, low]).astype(jnp.bfloat16)
    packed = jnp.repeat(jnp.concatenate([members, counts, parts], axis=0), copies, axis=1)
    got = lax.all_to_all(packed, "grid", 1, 2, tiled=True)[:, 0]
    split = got[count + 1 :].astype(jnp.float32)
    innov = split[0] + split[1] + split[2]
    precision = lax.dynamic_index_in_dim(obs_precision, level, 0, keepdims=False)
    weight = got[count].astype(jnp.float32) * precision
    widened = lax.optimization_barrier(got[:count]).astype(jnp.float32)
    span = nlat // copies
    own = lax.broadcasted_iota(jnp.int32, (nlat, nlon), 0) // span == grid_index % copies
    first = mem_index == 0
    half = grid_index % copies

    def own_rows(field):
        return lax.dynamic_slice_in_dim(field, half * span, span, axis=1)

    def squares(field):
        mine = own_rows(field)
        return jnp.sum(mine * mine, axis=(0, 1))

    def weighted(total):
        mine = lax.dynamic_slice_in_dim(total, half * span, span, axis=0)
        scale = lax.dynamic_slice_in_dim(weight, half * span, span, axis=0)
        return jnp.where(first, jnp.sum(scale * mine * mine, axis=0), 0.0)

    def by_target(field):
        return jnp.repeat(field.reshape(grid_size, rows, nlon), mem_size, axis=0)

    residual = smooth_rows(widened * (weight * innov)[None])
    total1 = mem_total(jnp.sum(widened * smooth_rows(residual), axis=0))
    image = residual + smooth_rows(widened * (weight * total1)[None])
    image_part = jnp.sum(widened * smooth_rows(image), axis=0)
    if copies > 1:
        rows_for = jnp.where(grid_index % copies == 0, by_target(total1), by_target(image_part))
    else:
        rows_for = jnp.concatenate([by_target(total1), by_target(image_part)], axis=1)
    sums1, got1 = exchange([squares(residual), weighted(total1)], rows_for)
    norm_now = sums1[0]
    curvature1 = sums1[1]
    step1 = norm_now / (norm_now + curvature1)
    if copies > 1:
        by_source = got1.reshape(levels, copies, mem_size, rows, nlon)
        total1_rows = by_source[:, 0, 0]
        image_rows = jnp.sum(by_source[:, 1], axis=1)
    else:
        by_source = got1.reshape(levels, mem_size, 2 * rows, nlon)
        total1_rows = by_source[:, 0, :rows]
        image_rows = jnp.sum(by_source[:, :, rows:], axis=1)
    residual_next = residual - step1 * image
    weight_rows = observed_count.astype(jnp.float32)[None] * obs_precision[:, None, None]
    moved_rows = total1_rows - step1 * image_rows
    sums, _ = exchange(
        [
            squares(residual_next),
            jnp.sum(own_rows(residual_next) * own_rows(residual), axis=(0, 1)),
            jnp.where(first, jnp.sum(weight_rows * moved_rows * moved_rows, axis=(0, 1)), 0.0),
            jnp.where(first, jnp.sum(weight_rows * moved_rows * total1_rows, axis=(0, 1)), 0.0),
        ],
        jnp.zeros((grid_size * mem_size, 0, nlon), jnp.float32),
        width=128,
    )
    norm_next = sums[0]
    beta = norm_next / norm_now
    direction_sq = norm_next + 2.0 * beta * sums[1] + beta * beta * norm_now
    curvature2 = sums[2] + 2.0 * beta * sums[3] + beta * beta * curvature1
    step2 = norm_next / (direction_sq + curvature2)
    total2_rows = moved_rows + beta * total1_rows
    whole = step1 * total1_rows + step2 * total2_rows
    share = levels // mem_size
    mine_out = lax.dynamic_slice_in_dim(whole, mem_index * share, share, 0)
    recentred = (members.astype(jnp.float32) + whole[None]).astype(jnp.bfloat16)
    return (recentred, mine_out)


def solution(mesh):
    placed = (P("mem", None, "grid", None), P(None, "grid", None), P("grid", None), P())
    grid_size, mem_size = (mesh.shape["grid"], mesh.shape["mem"])
    body = local

    def chosen(members, innovation, observed_count, obs_precision):
        levels = members.shape[1]
        fits = (
            grid_size % levels == 0
            and grid_size // levels <= 2
            and (levels % mem_size == 0)
            and (ITERS == 2)
        )
        pick = local_by_level if fits else body
        return jax.shard_map(
            pick,
            mesh=mesh,
            in_specs=placed,
            out_specs=(P("mem", None, "grid", None), P("mem", "grid", None)),
            check_vma=False,
        )(members, innovation, observed_count, obs_precision)

    return chosen
```

profile of v0, /device:TPU:0, one launch (start us, length us, event | category | flops | bytes accessed | tf_op | source)
XLA Modules:
  0.0 62.8 jit_solution(13325547275627384999)
XLA Ops:
  0.6 0.8 %fusion.80 = (bf16[2,512]{1,0:T(2,128)(2,1)S(1)}, f32[2,512]{1,0:T(2,128)S(1)}) fusion(s32[2,512]{1,0:T(2,128)} %param.6), kind=kLoop, calls=%fused_computation.179 | loop fusion | flops 2048 | bytes 10240 | tf_op jit(solution)/shard_map/convert_element_type | solution.py:119
  1.4 1.0 %constant_dynamic-update-slice_fusion.4 = bf16[24,4,2,512]{3,2,1,0:T(2,128)(2,1)S(1)} fusion(bf16[20,4,2,512]{3,2,1,0:T(2,128)(2,1)} %param.4), kind=kLoop, calls=%fused_computation.140 | loop fusion | bytes 327680
  2.7 0.9 %broadcast_in_dim.56 = bf16[24,4,2,2,512]{4,3,0,2,1:T(2,128)(2,1)} broadcast(bf16[24,4,2,512]{3,2,0,1:T(2,128)(2,1)S(1)} %copy.11), dimensions={0,1,3,4} | broadcast | bytes 589824 | tf_op jit(solution)/shard_map/broadcast_in_dim | solution.py:125
  3.6 7.3 %all-to-all-start = ((bf16[24,8,2,512]{3,2,0,1:T(2,128)(2,1)}), bf16[24,8,2,512]{3,2,0,1:T(2,128)(2,1)S(1)}, u32[]{:S(2)}, u32[]{:S(2)}) async-start(bf16[24,8,2,512]{3,2,0,1:T(2,128)(2,1)} %bitcast.3), calls=%async_computation | async-start | bytes 786432 | tf_op jit(solution)/shard_map/all_to_all | solution.py:126
  10.9 0.6 %copy-done.2 = f32[4]{0:T(128)S(1)} copy-done((f32[4]{0:T(128)S(1)}, f32[4]{0:T(128)}, u32[]{:S(2)}) %copy-start.2) | copy-done | bytes 40
  11.6 0.6 dynamic_slice.21
  12.2 10.4 %all-to-all-done = bf16[24,8,2,512]{3,2,0,1:T(2,128)(2,1)S(1)} async-done(((bf16[24,8,2,512]{3,2,0,1:T(2,128)(2,1)}), bf16[24,8,2,512]{3,2,0,1:T(2,128)(2,1)S(1)}, u32[]{:S(2)}, u32[]{:S(2)}) %all-to-all-start) | async-done | bytes 393248 | tf_op jit(solution)/shard_map/all_to_all | solution.py:126
  23.3 0.7 %convert_multiply_fusion.4 = (f32[1,8,2,512]{3,2,0,1:T(2,128)S(1)}, f32[1,8,2,512]{3,2,0,1:T(2,128)S(1)}) fusion(bf16[24,8,2,512]{3,2,0,1:T(2,128)(2,1)S(1)} %all-to-all-done, f32[]{:T(128)} %bitcast.4, f32[3,8,2,512]{3,2,0,1:T(2,128)S(1)} %slice_convert_fusion), kind=kLoop, calls=%fused_computation.117 | loop fusion | flops 40960 | bytes 180228 | tf_op jit(solution)/shard_map/mul | solution.py:130
  24.2 0.3 fusion.28
  24.6 0.9 %fusion.23 = f32[20,16,512]{2,1,0:T(8,128)S(1)} fusion(f32[20,16,512]{2,1,0:T(8,128)S(1)} %fusion.28, f32[20,16,2]{2,1,0:T(8,128)S(1)} %get-tuple-element.14, f32[20,16,2]{2,1,0:T(8,128)S(1)} %get-tuple-element.13), kind=kLoop, calls=%fused_computation.59 | loop fusion | flops 1802240 | bytes 1315840 | tf_op jit(solution)/shard_map/add | solution.py:87
  25.5 0.3 fusion.34
  26.0 0.9 %fusion.57 = f32[16,512]{1,0:T(8,128)S(1)} fusion(f32[20,16,2]{2,1,0:T(8,128)S(1)} %get-tuple-element.12, f32[20,16,512]{2,1,0:T(8,128)S(1)} %fusion.34, f32[20,16,2]{2,1,0:T(8,128)S(1)} %get-tuple-element.11, bf16[20,16,512]{2,1,0:T(8,128)(2,1)S(1)} %slice.194), kind=kLoop, calls=%fused_computation.101 | loop fusion | flops 2285568 | bytes 1020928 | tf_op jit(solution)/shard_map/reduce_sum | solution.py:153
  26.9 0.7 %broadcast_in_dim.57 = f32[4,16,512]{2,1,0:T(8,128)} broadcast(f32[16,512]{1,0:T(8,128)S(1)} %fusion.57), dimensions={1,2} | broadcast | bytes 163840 | tf_op jit(solution)/shard_map/broadcast_in_dim | solution.py:106
  27.5 3.3 %all-to-all-start.1 = ((f32[4,16,512]{2,1,0:T(8,128)}), f32[4,16,512]{2,1,0:T(8,128)S(1)}, u32[]{:S(2)}, u32[]{:S(2)}) async-start(f32[4,16,512]{2,1,0:T(8,128)} %broadcast_in_dim.57), calls=%async_computation.1 | async-start | bytes 262144 | tf_op jit(solution)/shard_map/all_to_all | solution.py:106
  30.9 4.5 %all-to-all-done.1 = f32[4,16,512]{2,1,0:T(8,128)S(1)} async-done(((f32[4,16,512]{2,1,0:T(8,128)}), f32[4,16,512]{2,1,0:T(8,128)S(1)}, u32[]{:S(2)}, u32[]{:S(2)}) %all-to-all-start.1) | async-done | bytes 131104 | tf_op jit(solution)/shard_map/all_to_all | solution.py:106
  35.6 0.3 fusion.40
  36.0 0.9 %fusion.11 = f32[20,16,512]{2,1,0:T(8,128)S(1)} fusion(f32[20,16,512]{2,1,0:T(8,128)S(1)} %fusion.23, f32[20,16,512]{2,1,0:T(8,128)S(1)} %fusion.40, f32[20,16,2]{2,1,0:T(8,128)S(1)} %get-tuple-element.10, f32[20,16,2]{2,1,0:T(8,128)S(1)} %get-tuple-element.9), kind=kLoop, calls=%fused_computation.47 | loop fusion | flops 1966080 | bytes 1971200 | tf_op jit(solution)/shard_map/add | solution.py:154
  37.4 0.9 %fusion.58 = f32[16,512]{1,0:T(8,128)S(1)} fusion(f32[20,16,2]{2,1,0:T(8,128)S(1)} %get-tuple-element.8, f32[20,16,512]{2,1,0:T(8,128)S(1)} %fusion.46, f32[20,16,2]{2,1,0:T(8,128)S(1)} %get-tuple-element.7, bf16[20,16,512]{2,1,0:T(8,128)(2,1)S(1)} %slice.194), kind=kLoop, calls=%fused_computation.102 | loop fusion | flops 2285568 | bytes 1020928 | tf_op jit(solution)/shard_map/reduce_sum | solution.py:155
  38.5 11.2 %all_to_all.32 = f32[32,1,1280]{2,1,0:T(1,128)S(1)} all-to-all(f32[32,1,1280]{2,1,0:T(1,128)S(1)} %all_to_all.24), channel_id=1, replica_groups=mesh['grid'=8,'mem'=4] {'grid','mem'}, dimensions={0} | all-to-all | bytes 327680 | tf_op jit(solution)/shard_map/all_to_all | solution.py:97
  50.3 0.7 %broadcast_in_dim.61 = f32[32,1,512]{2,1,0:T(1,128)} broadcast(f32[512]{0:T(512)S(1)} %pad_maximum_fusion.10), dimensions={2} | broadcast | bytes 67584 | tf_op jit(solution)/shard_map/broadcast_in_dim | solution.py:95
  51.0 2.7 %all-to-all-start.3 = ((f32[32,1,512]{2,1,0:T(1,128)}), f32[32,1,512]{2,1,0:T(1,128)S(1)}, u32[]{:S(2)}, u32[]{:S(2)}) async-start(f32[32,1,512]{2,1,0:T(1,128)} %broadcast_in_dim.61), calls=%async_computation.3 | async-start | bytes 131072 | tf_op jit(solution)/shard_map/all_to_all | solution.py:97
  53.7 7.4 %all-to-all-done.3 = f32[32,1,512]{2,1,0:T(1,128)S(1)} async-done(((f32[32,1,512]{2,1,0:T(1,128)}), f32[32,1,512]{2,1,0:T(1,128)S(1)}, u32[]{:S(2)}, u32[]{:S(2)}) %all-to-all-start.3) | async-done | bytes 65568 | tf_op jit(solution)/shard_map/all_to_all | solution.py:97
  61.4 0.8 %add_convert_fusion = bf16[20,4,2,512]{3,2,1,0:T(2,128)(2,1)} fusion(bf16[20,4,2,512]{3,2,1,0:T(2,128)(2,1)S(1)} %copy-done, f32[4,2,512]{2,1,0:T(2,128)S(1)} %multiply_add_fusion), kind=kLoop, calls=%fused_computation.105 | loop fusion | flops 245760 | bytes 344064 | tf_op jit(solution)/shard_map/convert_element_type | solution.py:194
  62.2 0.6 constant_dynamic-slice_fusion
  (55 shorter events, 3.1 us)
Async XLA Ops:
  1.4 1.1 %copy-start.1 = (f32[4,2,512]{2,1,0:T(2,128)S(1)}, f32[4,2,512]{2,1,0:T(2,128)}, u32[]{:S(2)}) copy-start(f32[4,2,512]{2,1,0:T(2,128)} %param.5) | copy-start | bytes 49156
  3.6 19.0 %all-to-all-start = ((bf16[24,8,2,512]{3,2,0,1:T(2,128)(2,1)}), bf16[24,8,2,512]{3,2,0,1:T(2,128)(2,1)S(1)}, u32[]{:S(2)}, u32[]{:S(2)}) async-start(bf16[24,8,2,512]{3,2,0,1:T(2,128)(2,1)} %bitcast.3), calls=%async_computation | async-start | bytes 786432 | tf_op jit(solution)/shard_map/all_to_all | solution.py:126
  10.9 0.7 %copy-start.2 = (f32[4]{0:T(128)S(1)}, f32[4]{0:T(128)}, u32[]{:S(2)}) copy-start(f32[4]{0:T(128)} %param.7) | copy-start | bytes 52
  27.5 7.9 %all-to-all-start.1 = ((f32[4,16,512]{2,1,0:T(8,128)}), f32[4,16,512]{2,1,0:T(8,128)S(1)}, u32[]{:S(2)}, u32[]{:S(2)}) async-start(f32[4,16,512]{2,1,0:T(8,128)} %broadcast_in_dim.57), calls=%async_computation.1 | async-start | bytes 262144 | tf_op jit(solution)/shard_map/all_to_all | solution.py:106
  51.0 10.4 %copy-start = (bf16[20,4,2,512]{3,2,1,0:T(2,128)(2,1)S(1)}, bf16[20,4,2,512]{3,2,1,0:T(2,128)(2,1)}, u32[]{:S(2)}) copy-start(bf16[20,4,2,512]{3,2,1,0:T(2,128)(2,1)} %param.4) | copy-start | bytes 491524
  51.0 10.1 %all-to-all-start.3 = ((f32[32,1,512]{2,1,0:T(1,128)}), f32[32,1,512]{2,1,0:T(1,128)S(1)}, u32[]{:S(2)}, u32[]{:S(2)}) async-start(f32[32,1,512]{2,1,0:T(1,128)} %broadcast_in_dim.61), calls=%async_computation.3 | async-start | bytes 131072 | tf_op jit(solution)/shard_map/all_to_all | solution.py:97
where the time goes:
time: 63.2 us; the launch traced here: 62.8 us
  waiting for transfers between devices  22.4 us (35%)
  starting transfers between devices  13.3 us (21%)
  blocking collectives  11.2 us (18%)
  other arithmetic  7.95 us (13%)
  local copies, waits for them, and re-layouts  6.78 us (11%)
  between operations  0.94 us (1%)
    all_to_all x1, blocking collectives, exchange(): got = lax.all_to_all(parcel, ('grid', 'mem'), 0, 0, tiled=True)  11.2 us
    all_to_all x1, waiting for transfers between devices, local_by_level(): got = lax.all_to_all(packed, 'grid', 1, 2, tiled=True)[:, 0]  10.4 us
    all_to_all x1, waiting for transfers between devices, exchange(): got = lax.all_to_all(parcel, ('grid', 'mem'), 0, 0, tiled=True)  7.41 us
    all_to_all x1, starting transfers between devices, local_by_level(): got = lax.all_to_all(packed, 'grid', 1, 2, tiled=True)[:, 0]  7.28 us
    all_to_all x1, waiting for transfers between devices, mem_total(): lax.all_to_all(jnp.broadcast_to(part, (mem_size,) + part.shape), 'mem', 0...  4.55 us
    all_to_all x1, starting transfers between devices, mem_total(): lax.all_to_all(jnp.broadcast_to(part, (mem_size,) + part.shape), 'mem', 0...  3.33 us
    all_to_all x1, starting transfers between devices, exchange(): got = lax.all_to_all(parcel, ('grid', 'mem'), 0, 0, tiled=True)  2.7 us
    unnamed x10, local copies, waits for them, and re-layouts  1.75 us
  transfers between devices with their start and end apart: 3, of which 3 were waited for; matrix products, arithmetic and copies ran while one was open for 1% of the time, Pallas kernels for 0%

commit v1 on v0

--- a/solution.py
+++ b/solution.py
@@ -108,6 +108,23 @@
 
 
 def local_by_level(members, innovation, observed_count, obs_precision):
+
+    def solve_roots(local_x):
+        carry_out = lax.axis_size("grid")
+        parts_out, small = (carry_out, lax.axis_index("grid"))
+        big = local_x.shape[1] // parts_out
+        wide_out = list(local_x.shape)
+        wide_out[1] = big
+        mixed_arr = wide_out[2]
+        wide_out[2] = mixed_arr * parts_out
+        y = jnp.zeros(wide_out, local_x.dtype)
+        for u in range(parts_out):
+            v_next = lax.dynamic_slice_in_dim(local_x, (small ^ u) * big, big, axis=1)
+            if u:
+                v_next = lax.ppermute(v_next, "grid", [(i0, i0 ^ u) for i0 in range(parts_out)])
+            y = lax.dynamic_update_slice_in_dim(y, v_next, (small ^ u) * mixed_arr, axis=2)
+        return y
+
     grid_size = lax.axis_size("grid")
     mem_size = lax.axis_size("mem")
     count, levels, rows, nlon = members.shape
@@ -123,7 +140,7 @@
     low = rest - middle
     parts = jnp.stack([high, middle, low]).astype(jnp.bfloat16)
     packed = jnp.repeat(jnp.concatenate([members, counts, parts], axis=0), copies, axis=1)
-    got = lax.all_to_all(packed, "grid", 1, 2, tiled=True)[:, 0]
+    got = solve_roots(packed)[:, 0]
     split = got[count + 1 :].astype(jnp.float32)
     innov = split[0] + split[1] + split[2]
     precision = lax.dynamic_index_in_dim(obs_precision, level, 0, keepdims=False)

time: 63.2 us -> 69.1 us (1.093)
  starting transfers between devices: 13.3 us -> 19.8 us
  waiting for transfers between devices: 22.4 us -> 19.3 us
  blocking collectives: 11.2 us -> 13.4 us
    ppermute x0 -> x7, starting transfers between devices: none -> 13.8 us  [solve_roots(): lax.ppermute(v_next, 'grid', [(i0, i0 ^ u) for i0 in range(parts_out)])]
    all_to_all x1 -> x0, waiting for transfers between devices: 10.4 us -> none  [local_by_level(): got = lax.all_to_all(packed, 'grid', 1, 2, tiled=True)[:, 0]]
    ppermute x0 -> x7, waiting for transfers between devices: none -> 7.29 us  [solve_roots(): lax.ppermute(v_next, 'grid', [(i0, i0 ^ u) for i0 in range(parts_out)])]
    all_to_all x1 -> x0, starting transfers between devices: 7.28 us -> none  [local_by_level(): got = lax.all_to_all(packed, 'grid', 1, 2, tiled=True)[:, 0]]
    all_to_all x1, blocking collectives: 11.2 us -> 13.4 us  [exchange(): got = lax.all_to_all(parcel, ('grid', 'mem'), 0, 0, tiled=True)]
    convert_element_type x1, other arithmetic: 0.77 us -> 0.01 us  [local_by_level(): observed_count.astype(jnp.bfloat16)]
    broadcast_in_dim x1, local copies, waits for them, and re-layouts: 0.94 us -> 0.21 us  [local_by_level(): jnp.repeat(jnp.concatenate([members, counts, parts], axis=0), copies, axi...]
    unnamed x10 -> x12, local copies, waits for them, and re-layouts: 1.75 us -> 2.42 us
  transfers between devices with their start and end apart: 3 -> 9, of which waited for: 3 -> 5; matrix products, arithmetic and copies ran while one was open for 1% -> 2% of each run, Pallas kernels for 0% -> 0%
where the time goes in v1:
time: 69.1 us; the launch traced here: 68.7 us
  starting transfers between devices  19.8 us (29%)
  waiting for transfers between devices  19.3 us (28%)
  blocking collectives  13.4 us (19%)
  other arithmetic  7.79 us (11%)
  local copies, waits for them, and re-layouts  6.89 us (10%)
  between operations  1.21 us (2%)
    ppermute x7, starting transfers between devices, solve_roots(): lax.ppermute(v_next, 'grid', [(i0, i0 ^ u) for i0 in range(parts_out)])  13.8 us
    all_to_all x1, blocking collectives, exchange(): got = lax.all_to_all(parcel, ('grid', 'mem'), 0, 0, tiled=True)  13.4 us
    all_to_all x1, waiting for transfers between devices, exchange(): got = lax.all_to_all(parcel, ('grid', 'mem'), 0, 0, tiled=True)  7.41 us
    ppermute x7, waiting for transfers between devices, solve_roots(): lax.ppermute(v_next, 'grid', [(i0, i0 ^ u) for i0 in range(parts_out)])  7.29 us
    all_to_all x1, waiting for transfers between devices, mem_total(): lax.all_to_all(jnp.broadcast_to(part, (mem_size,) + part.shape), 'mem', 0...  4.55 us
    all_to_all x1, starting transfers between devices, mem_total(): lax.all_to_all(jnp.broadcast_to(part, (mem_size,) + part.shape), 'mem', 0...  3.33 us
    all_to_all x1, starting transfers between devices, exchange(): got = lax.all_to_all(parcel, ('grid', 'mem'), 0, 0, tiled=True)  2.7 us
    unnamed x12, local copies, waits for them, and re-layouts  2.42 us
  transfers between devices with their start and end apart: 9, of which 5 were waited for; matrix products, arithmetic and copies ran while one was open for 2% of the time, Pallas kernels for 0%

profile of v1, /device:TPU:0, one launch (start us, length us, event | category | flops | bytes accessed | tf_op | source)
XLA Modules:
  0.0 68.7 jit_solution(4478329065446709864)
XLA Ops:
  0.7 0.7 copy-done.2
  1.4 1.0 %constant_dynamic-update-slice_fusion.4 = bf16[24,4,2,512]{3,2,1,0:T(2,128)(2,1)S(1)} fusion(bf16[20,4,2,512]{3,2,1,0:T(2,128)(2,1)} %param.4), kind=kLoop, calls=%fused_computation.151 | loop fusion | bytes 327680
  3.2 6.1 %collective-permute-start.6 = (bf16[24,1,2,512]{3,2,0,1:T(2,128)(2,1)S(1)}, bf16[24,1,2,512]{3,2,0,1:T(2,128)(2,1)S(1)}, u32[]{:S(2)}, u32[]{:S(2)}) collective-permute-start(bf16[24,1,2,512]{3,2,0,1:T(2,128)(2,1)S(1)} %get-tuple-element.17), channel_id=1, source_target_pairs={{0,28},{4,24},{8,20},{12,16},{16,12},{20,8},{24,4},{28,0},{1,29},{... | collective-permute-start | bytes 147464 | tf_op jit(solution)/shard_map/ppermute | solution.py:124
  9.4 0.8 %collective-permute-start.4 = (bf16[24,1,2,512]{3,2,0,1:T(2,128)(2,1)S(1)}, bf16[24,1,2,512]{3,2,0,1:T(2,128)(2,1)S(1)}, u32[]{:S(2)}, u32[]{:S(2)}) collective-permute-start(bf16[24,1,2,512]{3,2,0,1:T(2,128)(2,1)S(1)} %get-tuple-element.19), channel_id=1, source_target_pairs={{0,20},{4,16},{8,28},{12,24},{16,4},{20,0},{24,12},{28,8},{1,21},{... | collective-permute-start | bytes 147464 | tf_op jit(solution)/shard_map/ppermute | solution.py:124
  10.2 2.0 %collective-permute-start.3 = (bf16[24,1,2,512]{3,2,0,1:T(2,128)(2,1)S(1)}, bf16[24,1,2,512]{3,2,0,1:T(2,128)(2,1)S(1)}, u32[]{:S(2)}, u32[]{:S(2)}) collective-permute-start(bf16[24,1,2,512]{3,2,0,1:T(2,128)(2,1)S(1)} %get-tuple-element.20), channel_id=1, source_target_pairs={{0,16},{4,20},{8,24},{12,28},{16,0},{20,4},{24,8},{28,12},{1,17},{... | collective-permute-start | bytes 147464 | tf_op jit(solution)/shard_map/ppermute | solution.py:124
  12.2 1.6 %collective-permute-start = (bf16[24,1,2,512]{3,2,0,1:T(2,128)(2,1)S(1)}, bf16[24,1,2,512]{3,2,0,1:T(2,128)(2,1)S(1)}, u32[]{:S(2)}, u32[]{:S(2)}) collective-permute-start(bf16[24,1,2,512]{3,2,0,1:T(2,128)(2,1)S(1)} %get-tuple-element.23), channel_id=1, source_target_pairs={{0,4},{4,0},{8,12},{12,8},{16,20},{20,16},{24,28},{28,24},{1,5},{5... | collective-permute-start | bytes 147464 | tf_op jit(solution)/shard_map/ppermute | solution.py:124
  15.3 1.5 %collective-permute-done = bf16[24,1,2,512]{3,2,0,1:T(2,128)(2,1)S(1)} collective-permute-done((bf16[24,1,2,512]{3,2,0,1:T(2,128)(2,1)S(1)}, bf16[24,1,2,512]{3,2,0,1:T(2,128)(2,1)S(1)}, u32[]{:S(2)}, u32[]{:S(2)}) %collective-permute-start) | collective-permute-done | bytes 49184 | tf_op jit(solution)/shard_map/ppermute | solution.py:124
  16.8 0.9 %collective-permute-start.1 = (bf16[24,1,2,512]{3,2,0,1:T(2,128)(2,1)S(1)}, bf16[24,1,2,512]{3,2,0,1:T(2,128)(2,1)S(1)}, u32[]{:S(2)}, u32[]{:S(2)}) collective-permute-start(bf16[24,1,2,512]{3,2,0,1:T(2,128)(2,1)S(1)} %get-tuple-element.22), channel_id=1, source_target_pairs={{0,8},{4,12},{8,0},{12,4},{16,24},{20,28},{24,16},{28,20},{1,9},{5... | collective-permute-start | bytes 147464 | tf_op jit(solution)/shard_map/ppermute | solution.py:124
  17.8 3.1 %collective-permute-done.1 = bf16[24,1,2,512]{3,2,0,1:T(2,128)(2,1)S(1)} collective-permute-done((bf16[24,1,2,512]{3,2,0,1:T(2,128)(2,1)S(1)}, bf16[24,1,2,512]{3,2,0,1:T(2,128)(2,1)S(1)}, u32[]{:S(2)}, u32[]{:S(2)}) %collective-permute-start.1) | collective-permute-done | bytes 49184 | tf_op jit(solution)/shard_map/ppermute | solution.py:124
  20.9 2.2 %collective-permute-start.2 = (bf16[24,1,2,512]{3,2,0,1:T(2,128)(2,1)S(1)}, bf16[24,1,2,512]{3,2,0,1:T(2,128)(2,1)S(1)}, u32[]{:S(2)}, u32[]{:S(2)}) collective-permute-start(bf16[24,1,2,512]{3,2,0,1:T(2,128)(2,1)S(1)} %get-tuple-element.21), channel_id=1, source_target_pairs={{0,12},{4,8},{8,4},{12,0},{16,28},{20,24},{24,20},{28,16},{1,13},{... | collective-permute-start | bytes 147464 | tf_op jit(solution)/shard_map/ppermute | solution.py:124
  23.2 2.7 %collective-permute-done.2 = bf16[24,1,2,512]{3,2,0,1:T(2,128)(2,1)S(1)} collective-permute-done((bf16[24,1,2,512]{3,2,0,1:T(2,128)(2,1)S(1)}, bf16[24,1,2,512]{3,2,0,1:T(2,128)(2,1)S(1)}, u32[]{:S(2)}, u32[]{:S(2)}) %collective-permute-start.2) | collective-permute-done | bytes 49184 | tf_op jit(solution)/shard_map/ppermute | solution.py:124
  26.4 0.7 convert_multiply_fusion.4
  27.6 0.9 %fusion.23 = f32[20,16,512]{2,1,0:T(8,128)S(1)} fusion(f32[20,16,512]{2,1,0:T(8,128)S(1)} %fusion.28, f32[20,16,2]{2,1,0:T(8,128)S(1)} %get-tuple-element.14, f32[20,16,2]{2,1,0:T(8,128)S(1)} %get-tuple-element.13), kind=kLoop, calls=%fused_computation.59 | loop fusion | flops 1802240 | bytes 1315840 | tf_op jit(solution)/shard_map/add | solution.py:87
  28.9 0.9 %fusion.57 = f32[16,512]{1,0:T(8,128)S(1)} fusion(f32[20,16,2]{2,1,0:T(8,128)S(1)} %get-tuple-element.12, f32[20,16,512]{2,1,0:T(8,128)S(1)} %fusion.34, f32[20,16,2]{2,1,0:T(8,128)S(1)} %get-tuple-element.11, bf16[20,16,512]{2,1,0:T(8,128)(2,1)S(1)} %slice.240), kind=kLoop, calls=%fused_computation.101 | loop fusion | flops 2285568 | bytes 1020928 | tf_op jit(solution)/shard_map/reduce_sum | solution.py:170
  29.8 0.7 broadcast_in_dim.58
  30.5 3.3 %all-to-all-start = ((f32[4,16,512]{2,1,0:T(8,128)}), f32[4,16,512]{2,1,0:T(8,128)S(1)}, u32[]{:S(2)}, u32[]{:S(2)}) async-start(f32[4,16,512]{2,1,0:T(8,128)} %broadcast_in_dim.58), calls=%async_computation | async-start | bytes 262144 | tf_op jit(solution)/shard_map/all_to_all | solution.py:106
  33.9 4.5 %all-to-all-done = f32[4,16,512]{2,1,0:T(8,128)S(1)} async-done(((f32[4,16,512]{2,1,0:T(8,128)}), f32[4,16,512]{2,1,0:T(8,128)S(1)}, u32[]{:S(2)}, u32[]{:S(2)}) %all-to-all-start) | async-done | bytes 131104 | tf_op jit(solution)/shard_map/all_to_all | solution.py:106
  39.6 0.9 %fusion.11 = f32[20,16,512]{2,1,0:T(8,128)S(1)} fusion(f32[20,16,512]{2,1,0:T(8,128)S(1)} %fusion.23, f32[20,16,512]{2,1,0:T(8,128)S(1)} %fusion.40, f32[20,16,2]{2,1,0:T(8,128)S(1)} %get-tuple-element.10, f32[20,16,2]{2,1,0:T(8,128)S(1)} %get-tuple-element.9), kind=kLoop, calls=%fused_computation.47 | loop fusion | flops 1966080 | bytes 1971200 | tf_op jit(solution)/shard_map/add | solution.py:171
  41.0 0.9 %fusion.58 = f32[16,512]{1,0:T(8,128)S(1)} fusion(f32[20,16,2]{2,1,0:T(8,128)S(1)} %get-tuple-element.8, f32[20,16,512]{2,1,0:T(8,128)S(1)} %fusion.46, f32[20,16,2]{2,1,0:T(8,128)S(1)} %get-tuple-element.7, bf16[20,16,512]{2,1,0:T(8,128)(2,1)S(1)} %slice.240), kind=kLoop, calls=%fused_computation.102 | loop fusion | flops 2285568 | bytes 1020928 | tf_op jit(solution)/shard_map/reduce_sum | solution.py:172
  42.2 13.4 %all_to_all.23 = f32[32,1,1280]{2,1,0:T(1,128)S(1)} all-to-all(f32[32,1,1280]{2,1,0:T(1,128)S(1)} %all_to_all.16), channel_id=1, replica_groups=mesh['grid'=8,'mem'=4] {'grid','mem'}, dimensions={0} | all-to-all | bytes 327680 | tf_op jit(solution)/shard_map/all_to_all | solution.py:97
  56.2 0.7 broadcast_in_dim.62
  56.9 2.7 %all-to-all-start.2 = ((f32[32,1,512]{2,1,0:T(1,128)}), f32[32,1,512]{2,1,0:T(1,128)S(1)}, u32[]{:S(2)}, u32[]{:S(2)}) async-start(f32[32,1,512]{2,1,0:T(1,128)} %broadcast_in_dim.62), calls=%async_computation.2 | async-start | bytes 131072 | tf_op jit(solution)/shard_map/all_to_all | solution.py:97
  59.6 7.4 %all-to-all-done.2 = f32[32,1,512]{2,1,0:T(1,128)S(1)} async-done(((f32[32,1,512]{2,1,0:T(1,128)}), f32[32,1,512]{2,1,0:T(1,128)S(1)}, u32[]{:S(2)}, u32[]{:S(2)}) %all-to-all-start.2) | async-done | bytes 65568 | tf_op jit(solution)/shard_map/all_to_all | solution.py:97
  67.3 0.8 %add_convert_fusion = bf16[20,4,2,512]{3,2,1,0:T(2,128)(2,1)} fusion(bf16[20,4,2,512]{3,2,1,0:T(2,128)(2,1)S(1)} %copy-done, f32[4,2,512]{2,1,0:T(2,128)S(1)} %multiply_add_fusion), kind=kLoop, calls=%fused_computation.105 | loop fusion | flops 245760 | bytes 344064 | tf_op jit(solution)/shard_map/convert_element_type | solution.py:211
  (75 shorter events, 7.1 us)
Async XLA Ops:
  0.7 0.7 %copy-start.2 = (s32[2,512]{1,0:T(2,128)S(1)}, s32[2,512]{1,0:T(2,128)}, u32[]{:S(2)}) copy-start(s32[2,512]{1,0:T(2,128)} %param.6) | copy-start | bytes 12292
  1.4 1.1 %copy-start.1 = (f32[4,2,512]{2,1,0:T(2,128)S(1)}, f32[4,2,512]{2,1,0:T(2,128)}, u32[]{:S(2)}) copy-start(f32[4,2,512]{2,1,0:T(2,128)} %param.5) | copy-start | bytes 49156
  3.2 23.1 %collective-permute-start.6 = (bf16[24,1,2,512]{3,2,0,1:T(2,128)(2,1)S(1)}, bf16[24,1,2,512]{3,2,0,1:T(2,128)(2,1)S(1)}, u32[]{:S(2)}, u32[]{:S(2)}) collective-permute-start(bf16[24,1,2,512]{3,2,0,1:T(2,128)(2,1)S(1)} %get-tuple-element.17), channel_id=1, source_target_pairs={{0,28},{4,24},{8,20},{12,16},{16,12},{20,8},{24,4},{28,0},{1,29},{... | collective-permute-start | bytes 147464 | tf_op jit(solution)/shard_map/ppermute | solution.py:124
  9.2 16.9 %collective-permute-start.5 = (bf16[24,1,2,512]{3,2,0,1:T(2,128)(2,1)S(1)}, bf16[24,1,2,512]{3,2,0,1:T(2,128)(2,1)S(1)}, u32[]{:S(2)}, u32[]{:S(2)}) collective-permute-start(bf16[24,1,2,512]{3,2,0,1:T(2,128)(2,1)S(1)} %get-tuple-element.18), channel_id=1, source_target_pairs={{0,24},{4,28},{8,16},{12,20},{16,8},{20,12},{24,0},{28,4},{1,25},{... | collective-permute-start | bytes 147464 | tf_op jit(solution)/shard_map/ppermute | solution.py:124
  9.4 16.6 %collective-permute-start.4 = (bf16[24,1,2,512]{3,2,0,1:T(2,128)(2,1)S(1)}, bf16[24,1,2,512]{3,2,0,1:T(2,128)(2,1)S(1)}, u32[]{:S(2)}, u32[]{:S(2)}) collective-permute-start(bf16[24,1,2,512]{3,2,0,1:T(2,128)(2,1)S(1)} %get-tuple-element.19), channel_id=1, source_target_pairs={{0,20},{4,16},{8,28},{12,24},{16,4},{20,0},{24,12},{28,8},{1,21},{... | collective-permute-start | bytes 147464 | tf_op jit(solution)/shard_map/ppermute | solution.py:124
  10.2 15.7 %collective-permute-start.3 = (bf16[24,1,2,512]{3,2,0,1:T(2,128)(2,1)S(1)}, bf16[24,1,2,512]{3,2,0,1:T(2,128)(2,1)S(1)}, u32[]{:S(2)}, u32[]{:S(2)}) collective-permute-start(bf16[24,1,2,512]{3,2,0,1:T(2,128)(2,1)S(1)} %get-tuple-element.20), channel_id=1, source_target_pairs={{0,16},{4,20},{8,24},{12,28},{16,0},{20,4},{24,8},{28,12},{1,17},{... | collective-permute-start | bytes 147464 | tf_op jit(solution)/shard_map/ppermute | solution.py:124
  12.2 4.5 %collective-permute-start = (bf16[24,1,2,512]{3,2,0,1:T(2,128)(2,1)S(1)}, bf16[24,1,2,512]{3,2,0,1:T(2,128)(2,1)S(1)}, u32[]{:S(2)}, u32[]{:S(2)}) collective-permute-start(bf16[24,1,2,512]{3,2,0,1:T(2,128)(2,1)S(1)} %get-tuple-element.23), channel_id=1, source_target_pairs={{0,4},{4,0},{8,12},{12,8},{16,20},{20,16},{24,28},{28,24},{1,5},{5... | collective-permute-start | bytes 147464 | tf_op jit(solution)/shard_map/ppermute | solution.py:124
  14.1 0.7 copy-start.3
  16.8 4.1 %collective-permute-start.1 = (bf16[24,1,2,512]{3,2,0,1:T(2,128)(2,1)S(1)}, bf16[24,1,2,512]{3,2,0,1:T(2,128)(2,1)S(1)}, u32[]{:S(2)}, u32[]{:S(2)}) collective-permute-start(bf16[24,1,2,512]{3,2,0,1:T(2,128)(2,1)S(1)} %get-tuple-element.22), channel_id=1, source_target_pairs={{0,8},{4,12},{8,0},{12,4},{16,24},{20,28},{24,16},{28,20},{1,9},{5... | collective-permute-start | bytes 147464 | tf_op jit(solution)/shard_map/ppermute | solution.py:124
  20.9 5.0 %collective-permute-start.2 = (bf16[24,1,2,512]{3,2,0,1:T(2,128)(2,1)S(1)}, bf16[24,1,2,512]{3,2,0,1:T(2,128)(2,1)S(1)}, u32[]{:S(2)}, u32[]{:S(2)}) collective-permute-start(bf16[24,1,2,512]{3,2,0,1:T(2,128)(2,1)S(1)} %get-tuple-element.21), channel_id=1, source_target_pairs={{0,12},{4,8},{8,4},{12,0},{16,28},{20,24},{24,20},{28,16},{1,13},{... | collective-permute-start | bytes 147464 | tf_op jit(solution)/shard_map/ppermute | solution.py:124
  30.5 7.9 %all-to-all-start = ((f32[4,16,512]{2,1,0:T(8,128)}), f32[4,16,512]{2,1,0:T(8,128)S(1)}, u32[]{:S(2)}, u32[]{:S(2)}) async-start(f32[4,16,512]{2,1,0:T(8,128)} %broadcast_in_dim.58), calls=%async_computation | async-start | bytes 262144 | tf_op jit(solution)/shard_map/all_to_all | solution.py:106
  56.9 10.4 %copy-start = (bf16[20,4,2,512]{3,2,1,0:T(2,128)(2,1)S(1)}, bf16[20,4,2,512]{3,2,1,0:T(2,128)(2,1)}, u32[]{:S(2)}) copy-start(bf16[20,4,2,512]{3,2,1,0:T(2,128)(2,1)} %param.4) | copy-start | bytes 491524
  56.9 10.1 %all-to-all-start.2 = ((f32[32,1,512]{2,1,0:T(1,128)}), f32[32,1,512]{2,1,0:T(1,128)S(1)}, u32[]{:S(2)}, u32[]{:S(2)}) async-start(f32[32,1,512]{2,1,0:T(1,128)} %broadcast_in_dim.62), calls=%async_computation.2 | async-start | bytes 131072 | tf_op jit(solution)/shard_map/all_to_all | solution.py:97
